TPU v7x, 32 devices: a whole 2x2x4 slice. The times are simulated.
32 devices in a mesh: groups: 2 (over y), freq: 4 (over x, core), recv: 4 (over z).
Axes of the slice: x: 2, y: 2, z: 4, core: 2. Of those that a mesh axis runs over, the one named last changes fastest.
Arguments:
- operator: bfloat16 [4, 32, 512, 2048], P('groups', 'freq', 'recv'), parts along dimension 0, may hold values from -0.125 to 0.125
- recorded: float32 [4, 32, 8, 512], P('groups', 'freq', None, 'recv'), parts along dimension 0, may hold values from -18 to 18
- win_start: int32 [16, 16], P('groups'), parts along dimension 0, may hold values from 0 to 15
- win_end: int32 [16, 16], P('groups'), parts along dimension 0, may hold values from 17 to 32
Outputs:
- reflectivity: float32 [4, 32, 8, 2048], P('groups', 'freq', None, 'recv'), parts along dimension 0
- residual: float32 [4, 32, 8, 512], P('groups', 'freq', None, 'recv'), parts along dimension 0
There are 2 independent parts, one for each index of `groups`. A program takes and returns all parts, laid end to end along the dimension named above; each array names one. Nothing has to cross between parts.
All inputs are finite; a program needn't handle non-finite values.
Results may differ from a plain program's by a relative error of at most 0.013.
Values may be sent and summed in bfloat16 or wider, within the bound.
No kernel may reach another device: no remote copies, remote signals or barrier semaphores. Data moves between devices by JAX's collectives and lax.ppermute only.
A program may use at most 64 MiB of HBM per device.

v0:
```python
import math
import jax
import jax.numpy as jnp
from jax import lax
from jax.sharding import PartitionSpec as P

SBLK = 128
LINK_TYPE = jnp.float32
ITERS = 5


def high_dot(left, right):
    return jnp.dot(left, right, precision=lax.Precision.HIGHEST)


def dft_rows(row_ids, length):
    positions = jnp.arange(length, dtype=jnp.int32)
    phases = (row_ids[:, None] * positions[None, :] % length).astype(jnp.float32) * (
        2.0 * math.pi / length
    )
    normalizer = 1.0 / math.sqrt(length)
    return (jnp.cos(phases) * normalizer, jnp.sin(phases) * normalizer)


def window_mask(column_ids, src_local, win_start, win_end, length):
    blocks = win_start.shape[1]
    side_ids = column_ids // src_local
    source_ids = lax.axis_index("recv") * src_local + column_ids % src_local
    flat_ids = side_ids * blocks + source_ids // SBLK
    table_ids = jnp.arange(win_start.shape[0] * blocks, dtype=jnp.int32)
    matches = flat_ids[:, None] == table_ids[None, :]
    opening = jnp.sum(jnp.where(matches, win_start.reshape(-1)[None, :], 0), axis=1)
    closing = jnp.sum(jnp.where(matches, win_end.reshape(-1)[None, :], 0), axis=1)
    samples = jnp.arange(length, dtype=jnp.int32)[:, None]
    return ((samples >= opening[None, :]) & (samples < closing[None, :])).astype(jnp.float32)


def adjoint(res, real_operator, imag_operator):
    real_part = jnp.einsum(
        "fbr,frs->fbs", res[0], real_operator, preferred_element_type=jnp.float32
    ) + jnp.einsum("fbr,frs->fbs", res[1], imag_operator, preferred_element_type=jnp.float32)
    imag_part = jnp.einsum(
        "fbr,frs->fbs", res[1], real_operator, preferred_element_type=jnp.float32
    ) - jnp.einsum("fbr,frs->fbs", res[0], imag_operator, preferred_element_type=jnp.float32)
    return jnp.stack([real_part, imag_part])


def split_adjoint(values, real_operator, imag_operator):
    high, low = split_high_low(values)
    doubled = adjoint(jnp.concatenate([high, low], axis=2), real_operator, imag_operator)
    rows = values.shape[2]
    return doubled[:, :, :rows] + doubled[:, :, rows:]


def forward(direction, real_operator, imag_operator):
    real_part = jnp.einsum(
        "fbs,frs->fbr", direction[0], real_operator, preferred_element_type=jnp.float32
    ) - jnp.einsum("fbs,frs->fbr", direction[1], imag_operator, preferred_element_type=jnp.float32)
    imag_part = jnp.einsum(
        "fbs,frs->fbr", direction[0], imag_operator, preferred_element_type=jnp.float32
    ) + jnp.einsum("fbs,frs->fbr", direction[1], real_operator, preferred_element_type=jnp.float32)
    return jnp.stack([real_part, imag_part])


def split_high_low(values):
    high = lax.reduce_precision(values, exponent_bits=8, mantissa_bits=7)
    return (high.astype(jnp.bfloat16), (values - high).astype(jnp.bfloat16))


def split_parts(values):
    pieces = []
    for value in values:
        high = lax.reduce_precision(value, exponent_bits=8, mantissa_bits=7)
        rest = value - high
        middle = lax.reduce_precision(rest, exponent_bits=8, mantissa_bits=7)
        pieces += [high, middle, rest - middle]
    return jnp.stack(pieces)


def reduce_gather(partial):
    scattered = lax.psum_scatter(partial.astype(LINK_TYPE), "recv", scatter_dimension=3, tiled=True)
    flat = scattered.reshape(scattered.shape[0], scattered.shape[1], -1)
    return lax.all_gather(flat, "freq", axis=1, tiled=True).astype(jnp.float32)


def gather_sources(block, values):
    src_local = block.shape[-1]
    recv_size = lax.axis_size("recv")
    rows = jnp.concatenate(split_high_low(block.reshape(-1, src_local)))
    pieces = split_parts(values)
    extra = jnp.zeros((16, src_local), jnp.float32).at[0, : pieces.shape[0]].set(pieces)
    payload = jnp.concatenate([rows, extra.astype(jnp.bfloat16)])
    gathered = lax.all_gather(payload, "recv", axis=1, tiled=True)
    count = rows.shape[0]
    half = count // 2
    joined = gathered[:half].astype(jnp.float32) + gathered[half:count].astype(jnp.float32)
    full = joined.reshape(block.shape[:-1] + (recv_size * src_local,))
    tail = gathered[count].reshape(recv_size, src_local)[:, : pieces.shape[0]].astype(jnp.float32)
    sums = jnp.sum(tail.reshape(recv_size, len(values), 3), axis=(0, 2))
    return (full, sums)


def on_device(operator, recorded, win_start, win_end):
    freq_local = operator.shape[1]
    sources = operator.shape[3]
    right_sides = recorded.shape[2]
    src_local = sources // lax.axis_size("recv")
    total_freq = freq_local * lax.axis_size("freq")
    columns = right_sides * src_local
    real_operator = operator[0]
    imag_operator = operator[1]
    cos_all, sin_all = dft_rows(jnp.arange(total_freq, dtype=jnp.int32), total_freq)
    own_rows = lax.axis_index("freq") * freq_local + jnp.arange(freq_local, dtype=jnp.int32)
    cos_own, sin_own = dft_rows(own_rows, total_freq)
    window = window_mask(
        jnp.arange(columns, dtype=jnp.int32), src_local, win_start, win_end, total_freq
    )
    block_shape = (2, freq_local, right_sides, src_local)

    def to_time(spectrum):
        time_real = high_dot(cos_all.T, spectrum[0]) - high_dot(sin_all.T, spectrum[1])
        time_imag = high_dot(sin_all.T, spectrum[0]) + high_dot(cos_all.T, spectrum[1])
        return (time_real, time_imag)

    def to_own_freq(kept_real, kept_imag):
        real_part = high_dot(cos_own, kept_real) + high_dot(sin_own, kept_imag)
        imag_part = high_dot(cos_own, kept_imag) - high_dot(sin_own, kept_real)
        return jnp.stack([real_part, imag_part]).reshape(block_shape)

    gradient = reduce_gather(split_adjoint(recorded, real_operator, imag_operator))
    time_real, time_imag = to_time(gradient)
    kept_real = time_real * window
    kept_imag = time_imag * window
    kept_power = jnp.sum(kept_real * kept_real + kept_imag * kept_imag)
    direction_own = to_own_freq(kept_real, kept_imag)
    direction_all, sums = gather_sources(direction_own, [kept_power])
    direction_power = sums[0]
    reflect = jnp.zeros(block_shape, jnp.float32)
    residual = recorded
    for iteration in range(ITERS):
        image = forward(direction_all.astype(jnp.bfloat16), real_operator, imag_operator)
        if iteration < ITERS - 1:
            normal = reduce_gather(split_adjoint(image, real_operator, imag_operator))
            normal_real, normal_imag = to_time(normal)
            image_part = jnp.sum(kept_real * normal_real + kept_imag * normal_imag)
            masked_real = normal_real * window
            masked_imag = normal_imag * window
            change_own = to_own_freq(masked_real, masked_imag)
            values = [image_part] if iteration == 0 else [image_part, kept_power]
            change_all, sums = gather_sources(change_own, values)
            image_energy = sums[0]
            if iteration > 0:
                direction_power = sums[1]
            step_length = direction_power / (image_energy + 1e-06)
            reflect = reflect + step_length * direction_own
            residual = residual - step_length * image
            direction_all = direction_all - step_length * change_all
            direction_own = direction_own - step_length * change_own
            kept_real = kept_real - step_length * masked_real
            kept_imag = kept_imag - step_length * masked_imag
            kept_power = jnp.sum(kept_real * kept_real + kept_imag * kept_imag)
        else:
            own_power = jnp.where(lax.axis_index("freq") == 0, kept_power, 0.0)
            direction_power, image_energy = lax.psum(
                (own_power, jnp.sum(image * image)), ("freq", "recv")
            )
            step_length = direction_power / (image_energy + 1e-06)
            reflect = reflect + step_length * direction_own
            residual = residual - step_length * image
    return (reflect, residual)


def solution(mesh):
    return jax.shard_map(
        on_device,
        mesh=mesh,
        in_specs=(
            P("groups", "freq", "recv", None),
            P("groups", "freq", None, "recv"),
            P("groups", None),
            P("groups", None),
        ),
        out_specs=(P("groups", "freq", None, "recv"), P("groups", "freq", None, "recv")),
        check_vma=False,
    )
```

profile of v0, /device:TPU:0, one launch (start us, length us, event | category | flops | bytes accessed | tf_op | source)
XLA Modules:
  0.0 635.1 jit_solution(10183816585812269567)
XLA Ops:
  8.1 3.0 fusion.38
  11.1 3.4 fusion.40
  17.0 29.9 %reduce-scatter.6.cloned.1.call-done = f32[2,8,8,512]{3,2,1,0:T(8,128)} async-done(((f32[2,8,8,2048]{3,2,1,0:T(8,128)}), f32[2,8,8,512]{3,2,1,0:T(8,128)}) %reduce-scatter.6.cloned.1.call-update) | async-done | bytes 262160 | tf_op jit(solution)/shard_map/reduce_scatter | solution.py:81
  48.9 1.8 select_reduce_fusion.1
  50.8 13.8 %all-gather.11.cloned.1.call-done = f32[2,32,4096]{2,1,0:T(8,128)} async-done(((f32[2,8,4096]{2,1,0:T(8,128)}), f32[2,32,4096]{2,1,0:T(8,128)}) %all-gather.11.cloned.1.call-update) | async-done | bytes 1048592 | tf_op jit(solution)/shard_map/all_gather | solution.py:83
  68.0 1.8 fusion.1
  69.9 2.5 add_reduce_fusion.8
  80.4 28.9 %all-gather.13.cloned.1.call-done = bf16[272,2048]{1,0:T(8,128)(2,1)} async-done(((bf16[272,512]{1,0:T(8,128)(2,1)}), bf16[272,2048]{1,0:T(8,128)(2,1)}) %all-gather.13.cloned.1.call-update) | async-done | bytes 1114128 | tf_op jit(solution)/shard_map/all_gather | solution.py:93
  110.6 3.5 fusion.34
  114.1 3.4 fusion.36
  117.5 3.5 fusion.151
  121.1 3.4 fusion.145
  128.4 26.7 %reduce-scatter.8.cloned.1.call-done = f32[2,8,8,512]{3,2,1,0:T(8,128)} async-done(((f32[2,8,8,2048]{3,2,1,0:T(8,128)}), f32[2,8,8,512]{3,2,1,0:T(8,128)}) %reduce-scatter.8.cloned.1.call-update) | async-done | bytes 262160 | tf_op jit(solution)/shard_map/reduce_scatter | solution.py:81
  156.9 15.6 %all-gather.15.cloned.1.call-done = f32[2,32,4096]{2,1,0:T(8,128)} async-done(((f32[2,8,4096]{2,1,0:T(8,128)}), f32[2,32,4096]{2,1,0:T(8,128)}) %all-gather.15.cloned.1.call-update) | async-done | bytes 1048592 | tf_op jit(solution)/shard_map/all_gather | solution.py:83
  176.0 1.7 convolution_subtract_fusion.3
  177.8 2.4 add_reduce_fusion.7
  190.7 27.3 %all-gather.17.cloned.1.call-done = bf16[272,2048]{1,0:T(8,128)(2,1)} async-done(((bf16[272,512]{1,0:T(8,128)(2,1)}), bf16[272,2048]{1,0:T(8,128)(2,1)}) %all-gather.17.cloned.1.call-update) | async-done | bytes 1114128 | tf_op jit(solution)/shard_map/all_gather | solution.py:93
  220.7 2.0 fusion.606
  222.8 3.4 fusion.26
  226.2 3.5 fusion.28
  229.7 3.4 fusion.163
  238.3 26.7 %reduce-scatter.10.cloned.1.call-done = f32[2,8,8,512]{3,2,1,0:T(8,128)} async-done(((f32[2,8,8,2048]{3,2,1,0:T(8,128)}), f32[2,8,8,512]{3,2,1,0:T(8,128)}) %reduce-scatter.10.cloned.1.call-update) | async-done | bytes 262160 | tf_op jit(solution)/shard_map/reduce_scatter | solution.py:81
  266.8 15.9 %all-gather.19.cloned.1.call-done = f32[2,32,4096]{2,1,0:T(8,128)} async-done(((f32[2,8,4096]{2,1,0:T(8,128)}), f32[2,32,4096]{2,1,0:T(8,128)}) %all-gather.19.cloned.1.call-update) | async-done | bytes 1048592 | tf_op jit(solution)/shard_map/all_gather | solution.py:83
  286.1 1.8 convolution_subtract_fusion.2
  287.9 3.9 add_reduce_fusion.5
  307.4 28.9 %all-gather.21.cloned.1.call-done = bf16[272,2048]{1,0:T(8,128)(2,1)} async-done(((bf16[272,512]{1,0:T(8,128)(2,1)}), bf16[272,2048]{1,0:T(8,128)(2,1)}) %all-gather.21.cloned.1.call-update) | async-done | bytes 1114128 | tf_op jit(solution)/shard_map/all_gather | solution.py:93
  340.8 3.4 fusion.18
  344.2 3.5 fusion.20
  347.8 3.4 fusion.175
  356.3 26.7 %reduce-scatter.12.cloned.1.call-done = f32[2,8,8,512]{3,2,1,0:T(8,128)} async-done(((f32[2,8,8,2048]{3,2,1,0:T(8,128)}), f32[2,8,8,512]{3,2,1,0:T(8,128)}) %reduce-scatter.12.cloned.1.call-update) | async-done | bytes 262160 | tf_op jit(solution)/shard_map/reduce_scatter | solution.py:81
  384.9 15.8 %all-gather.23.cloned.1.call-done = f32[2,32,4096]{2,1,0:T(8,128)} async-done(((f32[2,8,4096]{2,1,0:T(8,128)}), f32[2,32,4096]{2,1,0:T(8,128)}) %all-gather.23.cloned.1.call-update) | async-done | bytes 1048592 | tf_op jit(solution)/shard_map/all_gather | solution.py:83
  404.1 1.7 convolution_subtract_fusion.1
  405.9 3.9 add_reduce_fusion.3
  422.7 28.9 %all-gather.25.cloned.1.call-done = bf16[272,2048]{1,0:T(8,128)(2,1)} async-done(((bf16[272,512]{1,0:T(8,128)(2,1)}), bf16[272,2048]{1,0:T(8,128)(2,1)}) %all-gather.25.cloned.1.call-update) | async-done | bytes 1114128 | tf_op jit(solution)/shard_map/all_gather | solution.py:93
  454.6 2.1 fusion.605
  456.7 3.5 fusion.10
  460.2 3.4 fusion.12
  463.6 3.4 fusion.187
  472.2 26.7 %reduce-scatter.14.cloned.1.call-done = f32[2,8,8,512]{3,2,1,0:T(8,128)} async-done(((f32[2,8,8,2048]{3,2,1,0:T(8,128)}), f32[2,8,8,512]{3,2,1,0:T(8,128)}) %reduce-scatter.14.cloned.1.call-update) | async-done | bytes 262160 | tf_op jit(solution)/shard_map/reduce_scatter | solution.py:81
  500.9 15.5 %all-gather.27.cloned.1.call-done = f32[2,32,4096]{2,1,0:T(8,128)} async-done(((f32[2,8,4096]{2,1,0:T(8,128)}), f32[2,32,4096]{2,1,0:T(8,128)}) %all-gather.27.cloned.1.call-update) | async-done | bytes 1048592 | tf_op jit(solution)/shard_map/all_gather | solution.py:83
  519.9 1.7 convolution_subtract_fusion
  521.6 3.9 add_reduce_fusion.1
  547.1 25.1 %all-gather.29.cloned.1.call-done = bf16[272,2048]{1,0:T(8,128)(2,1)} async-done(((bf16[272,512]{1,0:T(8,128)(2,1)}), bf16[272,2048]{1,0:T(8,128)(2,1)}) %all-gather.29.cloned.1.call-update) | async-done | bytes 1114128 | tf_op jit(solution)/shard_map/all_gather | solution.py:93
  576.6 3.4 fusion.2
  579.9 3.4 fusion.4
  583.3 3.5 fusion.199
  586.9 3.5 fusion.193
  592.7 32.6 %all-reduce.5 = (f32[]{:T(128)}, f32[]{:T(128)}) all-reduce(f32[]{:T(128)S(6)} %select_n.95, f32[]{:T(128)} %multiply_reduce_fusion), channel_id=1, replica_groups=mesh['groups'=2,'freq'=4,'recv'=4] {'freq','recv'}, use_global_device_ids=true, to_apply=%region_24.25 | all-reduce | flops 2 | bytes 16 | tf_op jit(solution)/shard_map/psum | solution.py:164
  (260 shorter events, 92.4 us)
Async XLA Ops:
  7.2 39.8 %reduce-scatter.6.cloned.1.call-start = ((), (), s32[]{:S(2)}) async-start(), calls=%async_computation.5 | async-start | bytes 1310720 | tf_op jit(solution)/shard_map/reduce_scatter | solution.py:81
  15.1 33.6 %copy-start.35 = (s32[8,16]{1,0:T(8,128)S(1)}, s32[8,16]{1,0:T(8,128)}, u32[]{:S(2)}) copy-start(s32[8,16]{1,0:T(8,128)} %param.16) | copy-start | bytes 1540
  15.1 33.7 %copy-start.36 = (s32[8,16]{1,0:T(8,128)S(1)}, s32[8,16]{1,0:T(8,128)}, u32[]{:S(2)}) copy-start(s32[8,16]{1,0:T(8,128)} %param.17) | copy-start | bytes 1540
  16.9 47.6 %all-gather.11.cloned.1.call-start = ((), (), s32[]{:S(2)}) async-start(), calls=%async_computation.6 | async-start | bytes 1310720 | tf_op jit(solution)/shard_map/all_gather | solution.py:83
  48.6 60.6 %all-gather.13.cloned.1.call-start = ((), (), s32[]{:S(2)}) async-start(), calls=%async_computation.7 | async-start | bytes 1392640 | tf_op jit(solution)/shard_map/all_gather | solution.py:93
  80.1 75.0 %reduce-scatter.8.cloned.1.call-start = ((), (), s32[]{:S(2)}) async-start(), calls=%async_computation.8 | async-start | bytes 1310720 | tf_op jit(solution)/shard_map/reduce_scatter | solution.py:81
  110.6 13.9 %slice-start = ((s8[8388608]{0:T(1024)(128)(4,1)}), s8[4194304]{0:T(1024)(128)(4,1)S(1)}, s32[]{:S(2)}) async-start(s8[8388608]{0:T(1024)(128)(4,1)} %bitcast.400), calls=%async_computation.20 | async-start | bytes 8388608
  128.4 44.2 %all-gather.15.cloned.1.call-start = ((), (), s32[]{:S(2)}) async-start(), calls=%async_computation.9 | async-start | bytes 1310720 | tf_op jit(solution)/shard_map/all_gather | solution.py:83
  156.9 61.1 %all-gather.17.cloned.1.call-start = ((), (), s32[]{:S(2)}) async-start(), calls=%async_computation.10 | async-start | bytes 1392640 | tf_op jit(solution)/shard_map/all_gather | solution.py:93
  180.2 42.6 %copy-start.2 = (f32[32,4096]{1,0:T(8,128)}, f32[32,4096]{1,0:T(8,128)S(1)}, u32[]{:S(2)}) copy-start(f32[32,4096]{1,0:T(8,128)S(1)} %get-tuple-element.111) | copy-start | bytes 1572868
  188.8 76.2 %reduce-scatter.10.cloned.1.call-start = ((), (), s32[]{:S(2)}) async-start(), calls=%async_computation.11 | async-start | bytes 1310720 | tf_op jit(solution)/shard_map/reduce_scatter | solution.py:81
  220.7 12.4 %slice-start.2 = ((s8[8388608]{0:T(1024)(128)(4,1)}), s8[4194304]{0:T(1024)(128)(4,1)S(1)}, s32[]{:S(2)}) async-start(s8[8388608]{0:T(1024)(128)(4,1)} %bitcast.402), calls=%async_computation.22 | async-start | bytes 8388608
  238.2 44.4 %all-gather.19.cloned.1.call-start = ((), (), s32[]{:S(2)}) async-start(), calls=%async_computation.12 | async-start | bytes 1310720 | tf_op jit(solution)/shard_map/all_gather | solution.py:83
  266.7 69.6 %all-gather.21.cloned.1.call-start = ((), (), s32[]{:S(2)}) async-start(), calls=%async_computation.13 | async-start | bytes 1392640 | tf_op jit(solution)/shard_map/all_gather | solution.py:93
  304.5 39.7 %copy-start.9 = (f32[8,4096]{1,0:T(8,128)}, f32[8,4096]{1,0:T(8,128)S(1)}, u32[]{:S(2)}) copy-start(f32[8,4096]{1,0:T(8,128)S(1)} %convolution_subtract_fusion.7) | copy-start | bytes 393220
  306.2 38.1 %copy-start.11 = (f32[8,4096]{1,0:T(8,128)}, f32[8,4096]{1,0:T(8,128)S(1)}, u32[]{:S(2)}) copy-start(f32[8,4096]{1,0:T(8,128)S(1)} %convolution_add_fusion.7) | copy-start | bytes 393220
  307.2 75.9 %reduce-scatter.12.cloned.1.call-start = ((), (), s32[]{:S(2)}) async-start(), calls=%async_computation.14 | async-start | bytes 1310720 | tf_op jit(solution)/shard_map/reduce_scatter | solution.py:81
  339.3 11.9 %slice-start.4 = ((s8[8388608]{0:T(1024)(128)(4,1)}), s8[4194304]{0:T(1024)(128)(4,1)S(1)}, s32[]{:S(2)}) async-start(s8[8388608]{0:T(1024)(128)(4,1)} %bitcast.404), calls=%async_computation.24 | async-start | bytes 8388608
  355.1 50.7 %copy-start.1 = (f32[32,4096]{1,0:T(8,128)S(1)}, f32[32,4096]{1,0:T(8,128)}, u32[]{:S(2)}) copy-start(f32[32,4096]{1,0:T(8,128)} %get-tuple-element.112) | copy-start | bytes 1572868
  356.3 44.3 %all-gather.23.cloned.1.call-start = ((), (), s32[]{:S(2)}) async-start(), calls=%async_computation.15 | async-start | bytes 1310720 | tf_op jit(solution)/shard_map/all_gather | solution.py:83
  384.8 66.8 %all-gather.25.cloned.1.call-start = ((), (), s32[]{:S(2)}) async-start(), calls=%async_computation.16 | async-start | bytes 1392640 | tf_op jit(solution)/shard_map/all_gather | solution.py:93
  420.9 33.6 %copy-start.13 = (f32[8,4096]{1,0:T(8,128)}, f32[8,4096]{1,0:T(8,128)S(1)}, u32[]{:S(2)}) copy-start(f32[8,4096]{1,0:T(8,128)S(1)} %convolution_subtract_fusion.6) | copy-start | bytes 393220
  421.5 33.1 %copy-start.15 = (f32[8,4096]{1,0:T(8,128)}, f32[8,4096]{1,0:T(8,128)S(1)}, u32[]{:S(2)}) copy-start(f32[8,4096]{1,0:T(8,128)S(1)} %convolution_add_fusion.6) | copy-start | bytes 393220
  422.4 76.4 %reduce-scatter.14.cloned.1.call-start = ((), (), s32[]{:S(2)}) async-start(), calls=%async_computation.17 | async-start | bytes 1310720 | tf_op jit(solution)/shard_map/reduce_scatter | solution.py:81
  454.6 12.4 %slice-start.6 = ((s8[8388608]{0:T(1024)(128)(4,1)}), s8[4194304]{0:T(1024)(128)(4,1)S(1)}, s32[]{:S(2)}) async-start(s8[8388608]{0:T(1024)(128)(4,1)} %bitcast.406), calls=%async_computation.26 | async-start | bytes 8388608
  456.6 10.3 %slice-start.7 = ((s8[8388608]{0:T(1024)(128)(4,1)}), s8[4194304]{0:T(1024)(128)(4,1)S(1)}, s32[]{:S(2)}) async-start(s8[8388608]{0:T(1024)(128)(4,1)} %bitcast.406), calls=%async_computation.27 | async-start | bytes 8388608
  472.1 44.3 %all-gather.27.cloned.1.call-start = ((), (), s32[]{:S(2)}) async-start(), calls=%async_computation.18 | async-start | bytes 1310720 | tf_op jit(solution)/shard_map/all_gather | solution.py:83
  500.6 71.6 %all-gather.29.cloned.1.call-start = ((), (), s32[]{:S(2)}) async-start(), calls=%async_computation.19 | async-start | bytes 1392640 | tf_op jit(solution)/shard_map/all_gather | solution.py:93
  525.6 17.7 %copy-start.6 = (f32[8,4096]{1,0:T(8,128)S(1)}, f32[8,4096]{1,0:T(8,128)}, u32[]{:S(2)}) copy-start(f32[8,4096]{1,0:T(8,128)} %copy-done.5) | copy-start | bytes 393220
  525.6 17.8 %copy-start.8 = (f32[8,4096]{1,0:T(8,128)S(1)}, f32[8,4096]{1,0:T(8,128)}, u32[]{:S(2)}) copy-start(f32[8,4096]{1,0:T(8,128)} %copy-done.7) | copy-start | bytes 393220
  525.6 17.9 %copy-start.10 = (f32[8,4096]{1,0:T(8,128)S(1)}, f32[8,4096]{1,0:T(8,128)}, u32[]{:S(2)}) copy-start(f32[8,4096]{1,0:T(8,128)} %copy-done.9) | copy-start | bytes 393220
  525.6 18.6 %copy-start.12 = (f32[8,4096]{1,0:T(8,128)S(1)}, f32[8,4096]{1,0:T(8,128)}, u32[]{:S(2)}) copy-start(f32[8,4096]{1,0:T(8,128)} %copy-done.11) | copy-start | bytes 393220
  525.6 19.3 %copy-start.14 = (f32[8,4096]{1,0:T(8,128)S(1)}, f32[8,4096]{1,0:T(8,128)}, u32[]{:S(2)}) copy-start(f32[8,4096]{1,0:T(8,128)} %copy-done.13) | copy-start | bytes 393220
  525.6 20.1 %copy-start.16 = (f32[8,4096]{1,0:T(8,128)S(1)}, f32[8,4096]{1,0:T(8,128)}, u32[]{:S(2)}) copy-start(f32[8,4096]{1,0:T(8,128)} %copy-done.15) | copy-start | bytes 393220
  583.3 7.1 %copy-start.3 = (f32[32,4096]{1,0:T(8,128)S(1)}, f32[32,4096]{1,0:T(8,128)}, u32[]{:S(2)}) copy-start(f32[32,4096]{1,0:T(8,128)} %get-tuple-element.72) | copy-start | bytes 1572868
  583.3 7.1 %copy-start.4 = (f32[32,4096]{1,0:T(8,128)S(1)}, f32[32,4096]{1,0:T(8,128)}, u32[]{:S(2)}) copy-start(f32[32,4096]{1,0:T(8,128)} %get-tuple-element.73) | copy-start | bytes 1572868
  586.8 39.7 %copy-start.25 = (f32[1,8,8,128]{3,2,1,0:T(8,128)S(1)}, f32[1,8,8,128]{3,2,1,0:T(8,128)}, u32[]{:S(2)}) copy-start(f32[1,8,8,128]{3,2,1,0:T(8,128)} %copy-done.24) | copy-start | bytes 98308
  586.8 39.7 %copy-start.27 = (f32[1,8,8,128]{3,2,1,0:T(8,128)S(1)}, f32[1,8,8,128]{3,2,1,0:T(8,128)}, u32[]{:S(2)}) copy-start(f32[1,8,8,128]{3,2,1,0:T(8,128)} %copy-done.26) | copy-start | bytes 98308
  586.8 39.7 %copy-start.29 = (f32[1,8,8,128]{3,2,1,0:T(8,128)S(1)}, f32[1,8,8,128]{3,2,1,0:T(8,128)}, u32[]{:S(2)}) copy-start(f32[1,8,8,128]{3,2,1,0:T(8,128)} %copy-done.28) | copy-start | bytes 98308
  586.8 39.7 %copy-start.31 = (f32[1,8,8,128]{3,2,1,0:T(8,128)S(1)}, f32[1,8,8,128]{3,2,1,0:T(8,128)}, u32[]{:S(2)}) copy-start(f32[1,8,8,128]{3,2,1,0:T(8,128)} %copy-done.30) | copy-start | bytes 98308
  586.8 39.7 %copy-start.33 = (f32[1,8,8,128]{3,2,1,0:T(8,128)S(1)}, f32[1,8,8,128]{3,2,1,0:T(8,128)}, u32[]{:S(2)}) copy-start(f32[1,8,8,128]{3,2,1,0:T(8,128)} %copy-done.32) | copy-start | bytes 98308
  586.8 39.7 %copy-start.34 = (f32[2,8,8,128]{3,2,1,0:T(8,128)S(1)}, f32[2,8,8,128]{3,2,1,0:T(8,128)}, u32[]{:S(2)}) copy-start(f32[2,8,8,128]{3,2,1,0:T(8,128)} %param.15) | copy-start | bytes 196612
  586.9 40.3 %copy-start.18 = (f32[2,8,8,512]{3,2,1,0:T(8,128)S(1)}, f32[2,8,8,512]{3,2,1,0:T(8,128)}, u32[]{:S(2)}) copy-start(f32[2,8,8,512]{3,2,1,0:T(8,128)} %copy-done.17) | copy-start | bytes 786436
  586.9 40.3 %copy-start.19 = (f32[1,8,8,512]{3,2,1,0:T(8,128)S(1)}, f32[1,8,8,512]{3,2,1,0:T(8,128)}, u32[]{:S(2)}) copy-start(f32[1,8,8,512]{3,2,1,0:T(8,128)} %copy.21) | copy-start | bytes 393220
  586.9 40.3 %copy-start.20 = (f32[1,8,8,512]{3,2,1,0:T(8,128)S(1)}, f32[1,8,8,512]{3,2,1,0:T(8,128)}, u32[]{:S(2)}) copy-start(f32[1,8,8,512]{3,2,1,0:T(8,128)} %copy.20) | copy-start | bytes 393220
  586.9 40.3 %copy-start.21 = (f32[1,8,8,512]{3,2,1,0:T(8,128)S(1)}, f32[1,8,8,512]{3,2,1,0:T(8,128)}, u32[]{:S(2)}) copy-start(f32[1,8,8,512]{3,2,1,0:T(8,128)} %copy.23) | copy-start | bytes 393220
  586.9 40.3 %copy-start.22 = (f32[1,8,8,512]{3,2,1,0:T(8,128)S(1)}, f32[1,8,8,512]{3,2,1,0:T(8,128)}, u32[]{:S(2)}) copy-start(f32[1,8,8,512]{3,2,1,0:T(8,128)} %copy.22) | copy-start | bytes 393220
  586.9 40.3 %copy-start.23 = (f32[1,8,8,512]{3,2,1,0:T(8,128)S(1)}, f32[1,8,8,512]{3,2,1,0:T(8,128)}, u32[]{:S(2)}) copy-start(f32[1,8,8,512]{3,2,1,0:T(8,128)} %copy.25) | copy-start | bytes 393220
  (12 other events, 39.5 us)
Sparse Core Ops, SparseCore 0:
  17.1 29.8 reduce-scatter.5
  49.1 15.3 all-gather.10
  80.2 29.0 all-gather.12
  128.5 26.6 reduce-scatter.7
  157.1 15.3 all-gather.14
  189.0 29.0 all-gather.16
  238.3 26.6 reduce-scatter.9
  267.2 15.3 all-gather.18
  307.3 29.0 all-gather.20
  356.4 26.6 reduce-scatter.11
  385.2 15.3 all-gather.22
  422.6 29.0 all-gather.24
  472.2 26.6 reduce-scatter.13
  501.0 15.3 all-gather.26
  543.2 29.0 all-gather.28
where the time goes:
time: 644 us; the launch traced here: 635 us
  waiting for transfers between devices  353 us (55%)
  matrix products  136 us (21%)
  between operations  61.4 us (10%)
  blocking collectives  32.6 us (5%)
  other arithmetic  28.9 us (4%)
  local copies, waits for them, and re-layouts  21.9 us (3%)
    all_gather x5, waiting for transfers between devices, gather_sources(): gathered = lax.all_gather(payload, 'recv', axis=1, tiled=True)  139 us
    reduce_scatter x5, waiting for transfers between devices, reduce_gather(): lax.psum_scatter(partial.astype(LINK_TYPE), 'recv', scatter_dimension=3,...  137 us
    all_gather x5, waiting for transfers between devices, reduce_gather(): return lax.all_gather(flat, 'freq', axis=1, tiled=True).astype(jnp.float32)  76.5 us
    dot_general x40, matrix products, high_dot(): return jnp.dot(left, right, precision=lax.Precision.HIGHEST)  55 us
    psum x1, blocking collectives, on_device(): lax.psum((own_power, jnp.sum(image * image)), ('freq', 'recv'))  32.6 us
    dot_general x5, matrix products, forward(): jnp.einsum('fbs,frs->fbr', direction[1], imag_operator, preferred_element...  17.2 us
    dot_general x5, matrix products, forward(): jnp.einsum('fbs,frs->fbr', direction[1], real_operator, preferred_element...  17.2 us
    dot_general x5, matrix products, forward(): jnp.einsum('fbs,frs->fbr', direction[0], imag_operator, preferred_element...  17.2 us
  transfers between devices with their start and end apart: 15, of which 15 were waited for; matrix products, arithmetic and copies ran while one was open for 1% of the time, Pallas kernels for 0%

commit v1 on v0

--- a/solution.py
+++ b/solution.py
@@ -7,6 +7,24 @@
 SBLK = 128
 LINK_TYPE = jnp.float32
 ITERS = 5
+
+
+def in_order(blocks, dim):
+    blocks = jnp.moveaxis(blocks, 0, dim)
+    shape = blocks.shape
+    return blocks.reshape(*shape[:dim], shape[dim] * shape[dim + 1], *shape[dim + 2 :])
+
+
+def grow_blocks(x, axis):
+    peers = lax.axis_size(axis)
+    blocks = x[None]
+    for level in range(peers.bit_length() - 1):
+        bit = 1 << level
+        received = lax.ppermute(blocks, axis, [(i, i ^ bit) for i in range(peers)])
+        both = jnp.stack([blocks, received])
+        upper = lax.axis_index(axis) >> level & 1
+        blocks = jnp.where(upper == 0, both, both[::-1]).reshape(-1, *x.shape)
+    return blocks
 
 
 def high_dot(left, right):
@@ -90,7 +108,7 @@
     pieces = split_parts(values)
     extra = jnp.zeros((16, src_local), jnp.float32).at[0, : pieces.shape[0]].set(pieces)
     payload = jnp.concatenate([rows, extra.astype(jnp.bfloat16)])
-    gathered = lax.all_gather(payload, "recv", axis=1, tiled=True)
+    gathered = in_order(grow_blocks(payload, "recv"), 1)
     count = rows.shape[0]
     half = count // 2
     joined = gathered[:half].astype(jnp.float32) + gathered[half:count].astype(jnp.float32)

time: 644 us -> 701 us (1.089)
  starting transfers between devices: 1.88 us -> 20.5 us
  matrix products: 136 us -> 152 us
  local copies, waits for them, and re-layouts: 21.9 us -> 34.2 us
  waiting for transfers between devices: 353 us -> 365 us
    ppermute x0 -> x10, waiting for transfers between devices: none -> 150 us  [grow_blocks(): received = lax.ppermute(blocks, axis, [(i, i ^ bit) for i in range(peers)])]
    all_gather x5 -> x0, waiting for transfers between devices: 139 us -> none  [gather_sources(): gathered = lax.all_gather(payload, 'recv', axis=1, tiled=True)]
    ppermute x0 -> x10, starting transfers between devices: none -> 20.1 us  [grow_blocks(): received = lax.ppermute(blocks, axis, [(i, i ^ bit) for i in range(peers)])]
    dot_general x5, matrix products: 5.64 us -> 14.4 us  [adjoint(): jnp.einsum('fbr,frs->fbs', res[0], imag_operator, preferred_element_type=...]
  transfers between devices with their start and end apart: 15 -> 20, of which waited for: 15 -> 20; matrix products, arithmetic and copies ran while one was open for 1% -> 2% of each run, Pallas kernels for 0% -> 0%
where the time goes in v1:
time: 701 us; the launch traced here: 695 us
  waiting for transfers between devices  365 us (52%)
  matrix products  152 us (22%)
  between operations  62.6 us (9%)
  local copies, waits for them, and re-layouts  34.2 us (5%)
  blocking collectives  33.2 us (5%)
  other arithmetic  28.1 us (4%)
  starting transfers between devices  20.5 us (3%)
    ppermute x10, waiting for transfers between devices, grow_blocks(): received = lax.ppermute(blocks, axis, [(i, i ^ bit) for i in range(peers)])  150 us
    reduce_scatter x5, waiting for transfers between devices, reduce_gather(): lax.psum_scatter(partial.astype(LINK_TYPE), 'recv', scatter_dimension=3,...  139 us
    all_gather x5, waiting for transfers between devices, reduce_gather(): return lax.all_gather(flat, 'freq', axis=1, tiled=True).astype(jnp.float32)  76.2 us
    dot_general x40, matrix products, high_dot(): return jnp.dot(left, right, precision=lax.Precision.HIGHEST)  54.7 us
    psum x1, blocking collectives, on_device(): lax.psum((own_power, jnp.sum(image * image)), ('freq', 'recv'))  33.2 us
    ppermute x10, starting transfers between devices, grow_blocks(): received = lax.ppermute(blocks, axis, [(i, i ^ bit) for i in range(peers)])  20.1 us
    dot_general x5, matrix products, forward(): jnp.einsum('fbs,frs->fbr', direction[1], real_operator, preferred_element...  17.6 us
    dot_general x5, matrix products, forward(): jnp.einsum('fbs,frs->fbr', direction[0], imag_operator, preferred_element...  17.4 us
  transfers between devices with their start and end apart: 20, of which 20 were waited for; matrix products, arithmetic and copies ran while one was open for 2% of the time, Pallas kernels for 0%

profile of v1, /device:TPU:0, one launch (start us, length us, event | category | flops | bytes accessed | tf_op | source)
XLA Modules:
  0.0 695.5 jit_solution(3872600486575029293)
XLA Ops:
  8.1 3.0 fusion.38
  11.1 3.4 fusion.40
  17.0 29.9 %reduce-scatter.6.cloned.1.call-done = f32[2,8,8,512]{3,2,1,0:T(8,128)} async-done(((f32[2,8,8,2048]{3,2,1,0:T(8,128)}), f32[2,8,8,512]{3,2,1,0:T(8,128)}) %reduce-scatter.6.cloned.1.call-update) | async-done | bytes 262160 | tf_op jit(solution)/shard_map/reduce_scatter | solution.py:99
  51.2 13.3 %all-gather.6.cloned.1.call-done = f32[2,32,4096]{2,1,0:T(8,128)} async-done(((f32[2,8,4096]{2,1,0:T(8,128)}), f32[2,32,4096]{2,1,0:T(8,128)}) %all-gather.6.cloned.1.call-update) | async-done | bytes 1048592 | tf_op jit(solution)/shard_map/all_gather | solution.py:101
  81.0 7.3 %collective-permute-done = bf16[1,272,512]{2,1,0:T(8,128)(2,1)S(1)} collective-permute-done((bf16[1,272,512]{2,1,0:T(8,128)(2,1)S(1)}, bf16[1,272,512]{2,1,0:T(8,128)(2,1)S(1)}, u32[]{:S(2)}, u32[]{:S(2)}) %collective-permute-start) | collective-permute-done | bytes 278560 | tf_op jit(solution)/shard_map/ppermute | solution.py:23
  90.9 24.5 %collective-permute-done.1 = bf16[2,272,512]{2,1,0:T(8,128)(2,1)} collective-permute-done((bf16[2,272,512]{2,1,0:T(8,128)(2,1)S(1)}, bf16[2,272,512]{2,1,0:T(8,128)(2,1)}, u32[]{:S(2)}, u32[]{:S(2)}) %collective-permute-start.1) | collective-permute-done | bytes 557088 | tf_op jit(solution)/shard_map/ppermute | solution.py:23
  119.4 3.4 fusion.36
  123.0 3.5 fusion.34
  126.5 3.4 fusion.145
  129.9 3.5 fusion.151
  133.4 2.8 fusion.30
  139.8 27.2 %reduce-scatter.8.cloned.1.call-done = f32[2,8,8,512]{3,2,1,0:T(8,128)} async-done(((f32[2,8,8,2048]{3,2,1,0:T(8,128)}), f32[2,8,8,512]{3,2,1,0:T(8,128)}) %reduce-scatter.8.cloned.1.call-update) | async-done | bytes 262160 | tf_op jit(solution)/shard_map/reduce_scatter | solution.py:99
  168.8 15.6 %all-gather.8.cloned.1.call-done = f32[2,32,4096]{2,1,0:T(8,128)} async-done(((f32[2,8,4096]{2,1,0:T(8,128)}), f32[2,32,4096]{2,1,0:T(8,128)}) %all-gather.8.cloned.1.call-update) | async-done | bytes 1048592 | tf_op jit(solution)/shard_map/all_gather | solution.py:101
  201.6 7.3 %collective-permute-done.2 = bf16[1,272,512]{2,1,0:T(8,128)(2,1)S(1)} collective-permute-done((bf16[1,272,512]{2,1,0:T(8,128)(2,1)S(1)}, bf16[1,272,512]{2,1,0:T(8,128)(2,1)S(1)}, u32[]{:S(2)}, u32[]{:S(2)}) %collective-permute-start.2) | collective-permute-done | bytes 278560 | tf_op jit(solution)/shard_map/ppermute | solution.py:23
  212.8 23.1 %collective-permute-done.3 = bf16[2,272,512]{2,1,0:T(8,128)(2,1)S(1)} collective-permute-done((bf16[2,272,512]{2,1,0:T(8,128)(2,1)S(1)}, bf16[2,272,512]{2,1,0:T(8,128)(2,1)S(1)}, u32[]{:S(2)}, u32[]{:S(2)}) %collective-permute-start.3) | collective-permute-done | bytes 557088 | tf_op jit(solution)/shard_map/ppermute | solution.py:23
  244.3 3.4 fusion.28
  248.8 3.5 fusion.26
  252.4 3.4 fusion.157
  255.7 3.5 fusion.163
  265.9 27.2 %reduce-scatter.10.cloned.1.call-done = f32[2,8,8,512]{3,2,1,0:T(8,128)} async-done(((f32[2,8,8,2048]{3,2,1,0:T(8,128)}), f32[2,8,8,512]{3,2,1,0:T(8,128)}) %reduce-scatter.10.cloned.1.call-update) | async-done | bytes 262160 | tf_op jit(solution)/shard_map/reduce_scatter | solution.py:99
  294.9 15.7 %all-gather.10.cloned.1.call-done = f32[2,32,4096]{2,1,0:T(8,128)} async-done(((f32[2,8,4096]{2,1,0:T(8,128)}), f32[2,32,4096]{2,1,0:T(8,128)}) %all-gather.10.cloned.1.call-update) | async-done | bytes 1048592 | tf_op jit(solution)/shard_map/all_gather | solution.py:101
  315.9 3.9 add_reduce_fusion.5
  336.0 7.3 %collective-permute-done.4 = bf16[1,272,512]{2,1,0:T(8,128)(2,1)S(1)} collective-permute-done((bf16[1,272,512]{2,1,0:T(8,128)(2,1)S(1)}, bf16[1,272,512]{2,1,0:T(8,128)(2,1)S(1)}, u32[]{:S(2)}, u32[]{:S(2)}) %collective-permute-start.4) | collective-permute-done | bytes 278560 | tf_op jit(solution)/shard_map/ppermute | solution.py:23
  345.9 24.4 %collective-permute-done.5 = bf16[2,272,512]{2,1,0:T(8,128)(2,1)S(1)} collective-permute-done((bf16[2,272,512]{2,1,0:T(8,128)(2,1)S(1)}, bf16[2,272,512]{2,1,0:T(8,128)(2,1)S(1)}, u32[]{:S(2)}, u32[]{:S(2)}) %collective-permute-start.5) | collective-permute-done | bytes 557088 | tf_op jit(solution)/shard_map/ppermute | solution.py:23
  376.7 3.4 fusion.20
  380.3 3.5 fusion.18
  383.8 3.4 fusion.169
  387.2 3.5 fusion.175
  397.1 27.2 %reduce-scatter.12.cloned.1.call-done = f32[2,8,8,512]{3,2,1,0:T(8,128)} async-done(((f32[2,8,8,2048]{3,2,1,0:T(8,128)}), f32[2,8,8,512]{3,2,1,0:T(8,128)}) %reduce-scatter.12.cloned.1.call-update) | async-done | bytes 262160 | tf_op jit(solution)/shard_map/reduce_scatter | solution.py:99
  426.1 15.8 %all-gather.12.cloned.1.call-done = f32[2,32,4096]{2,1,0:T(8,128)} async-done(((f32[2,8,4096]{2,1,0:T(8,128)}), f32[2,32,4096]{2,1,0:T(8,128)}) %all-gather.12.cloned.1.call-update) | async-done | bytes 1048592 | tf_op jit(solution)/shard_map/all_gather | solution.py:101
  447.2 3.9 add_reduce_fusion.3
  464.8 7.3 %collective-permute-done.6 = bf16[1,272,512]{2,1,0:T(8,128)(2,1)S(1)} collective-permute-done((bf16[1,272,512]{2,1,0:T(8,128)(2,1)S(1)}, bf16[1,272,512]{2,1,0:T(8,128)(2,1)S(1)}, u32[]{:S(2)}, u32[]{:S(2)}) %collective-permute-start.6) | collective-permute-done | bytes 278560 | tf_op jit(solution)/shard_map/ppermute | solution.py:23
  474.8 24.4 %collective-permute-done.7 = bf16[2,272,512]{2,1,0:T(8,128)(2,1)S(1)} collective-permute-done((bf16[2,272,512]{2,1,0:T(8,128)(2,1)S(1)}, bf16[2,272,512]{2,1,0:T(8,128)(2,1)S(1)}, u32[]{:S(2)}, u32[]{:S(2)}) %collective-permute-start.7) | collective-permute-done | bytes 557088 | tf_op jit(solution)/shard_map/ppermute | solution.py:23
  503.5 3.0 fusion.625
  506.9 3.4 fusion.12
  510.4 3.5 fusion.10
  514.0 3.4 fusion.181
  517.3 3.5 fusion.187
  527.3 27.2 %reduce-scatter.14.cloned.1.call-done = f32[2,8,8,512]{3,2,1,0:T(8,128)} async-done(((f32[2,8,8,2048]{3,2,1,0:T(8,128)}), f32[2,8,8,512]{3,2,1,0:T(8,128)}) %reduce-scatter.14.cloned.1.call-update) | async-done | bytes 262160 | tf_op jit(solution)/shard_map/reduce_scatter | solution.py:99
  556.2 15.7 %all-gather.14.cloned.1.call-done = f32[2,32,4096]{2,1,0:T(8,128)} async-done(((f32[2,8,4096]{2,1,0:T(8,128)}), f32[2,32,4096]{2,1,0:T(8,128)}) %all-gather.14.cloned.1.call-update) | async-done | bytes 1048592 | tf_op jit(solution)/shard_map/all_gather | solution.py:101
  577.2 3.6 add_reduce_fusion.1
  594.5 7.3 %collective-permute-done.8 = bf16[1,272,512]{2,1,0:T(8,128)(2,1)S(1)} collective-permute-done((bf16[1,272,512]{2,1,0:T(8,128)(2,1)S(1)}, bf16[1,272,512]{2,1,0:T(8,128)(2,1)S(1)}, u32[]{:S(2)}, u32[]{:S(2)}) %collective-permute-start.8) | collective-permute-done | bytes 278560 | tf_op jit(solution)/shard_map/ppermute | solution.py:23
  612.6 17.3 %collective-permute-done.9 = bf16[2,272,512]{2,1,0:T(8,128)(2,1)} collective-permute-done((bf16[2,272,512]{2,1,0:T(8,128)(2,1)}, bf16[2,272,512]{2,1,0:T(8,128)(2,1)}, u32[]{:S(2)}, u32[]{:S(2)}) %collective-permute-start.9) | collective-permute-done | bytes 557088 | tf_op jit(solution)/shard_map/ppermute | solution.py:23
  635.1 3.4 fusion.4
  638.6 3.4 fusion.2
  642.0 3.5 fusion.193
  645.6 3.5 fusion.199
  651.4 33.2 %all-reduce.5 = (f32[]{:T(128)}, f32[]{:T(128)}) all-reduce(f32[]{:T(128)S(6)} %select_n.155, f32[]{:T(128)} %multiply_reduce_fusion), channel_id=1, replica_groups=mesh['groups'=2,'freq'=4,'recv'=4] {'freq','recv'}, use_global_device_ids=true, to_apply=%region_24.25 | all-reduce | flops 2 | bytes 16 | tf_op jit(solution)/shard_map/psum | solution.py:182
  (322 shorter events, 142.0 us)
Async XLA Ops:
  7.2 39.8 %reduce-scatter.6.cloned.1.call-start = ((), (), s32[]{:S(2)}) async-start(), calls=%async_computation.5 | async-start | bytes 1310720 | tf_op jit(solution)/shard_map/reduce_scatter | solution.py:99
  15.1 33.6 %copy-start.46 = (s32[8,16]{1,0:T(8,128)S(1)}, s32[8,16]{1,0:T(8,128)}, u32[]{:S(2)}) copy-start(s32[8,16]{1,0:T(8,128)} %param.16) | copy-start | bytes 1540
  15.1 33.7 %copy-start.47 = (s32[8,16]{1,0:T(8,128)S(1)}, s32[8,16]{1,0:T(8,128)}, u32[]{:S(2)}) copy-start(s32[8,16]{1,0:T(8,128)} %param.17) | copy-start | bytes 1540
  17.0 47.6 %all-gather.6.cloned.1.call-start = ((), (), s32[]{:S(2)}) async-start(), calls=%async_computation.6 | async-start | bytes 1310720 | tf_op jit(solution)/shard_map/all_gather | solution.py:101
  48.7 118.3 %reduce-scatter.8.cloned.1.call-start = ((), (), s32[]{:S(2)}) async-start(), calls=%async_computation.7 | async-start | bytes 1310720 | tf_op jit(solution)/shard_map/reduce_scatter | solution.py:99
  79.4 8.9 %collective-permute-start = (bf16[1,272,512]{2,1,0:T(8,128)(2,1)S(1)}, bf16[1,272,512]{2,1,0:T(8,128)(2,1)S(1)}, u32[]{:S(2)}, u32[]{:S(2)}) collective-permute-start(bf16[1,272,512]{2,1,0:T(8,128)(2,1)S(1)} %get-tuple-element.111), channel_id=1, source_target_pairs={{0,1},{1,0},{2,3},{3,2},{4,5},{5,4},{6,7},{7,6},{8,9},{9,8},{10,11... | collective-permute-start | bytes 835592 | tf_op jit(solution)/shard_map/ppermute | solution.py:23
  88.5 27.0 %collective-permute-start.1 = (bf16[2,272,512]{2,1,0:T(8,128)(2,1)S(1)}, bf16[2,272,512]{2,1,0:T(8,128)(2,1)}, u32[]{:S(2)}, u32[]{:S(2)}) collective-permute-start(bf16[2,272,512]{2,1,0:T(8,128)(2,1)S(1)} %get-tuple-element.91), channel_id=1, source_target_pairs={{0,2},{1,3},{2,0},{3,1},{4,6},{5,7},{6,4},{7,5},{8,10},{9,11},{10,... | collective-permute-start | bytes 1671176 | tf_op jit(solution)/shard_map/ppermute | solution.py:23
  139.7 44.7 %all-gather.8.cloned.1.call-start = ((), (), s32[]{:S(2)}) async-start(), calls=%async_computation.8 | async-start | bytes 1310720 | tf_op jit(solution)/shard_map/all_gather | solution.py:101
  168.7 124.4 %reduce-scatter.10.cloned.1.call-start = ((), (), s32[]{:S(2)}) async-start(), calls=%async_computation.9 | async-start | bytes 1310720 | tf_op jit(solution)/shard_map/reduce_scatter | solution.py:99
  192.1 43.9 %copy-start.7 = (f32[32,4096]{1,0:T(8,128)}, f32[32,4096]{1,0:T(8,128)S(1)}, u32[]{:S(2)}) copy-start(f32[32,4096]{1,0:T(8,128)S(1)} %get-tuple-element.141) | copy-start | bytes 1572868
  200.0 8.9 %collective-permute-start.2 = (bf16[1,272,512]{2,1,0:T(8,128)(2,1)S(1)}, bf16[1,272,512]{2,1,0:T(8,128)(2,1)S(1)}, u32[]{:S(2)}, u32[]{:S(2)}) collective-permute-start(bf16[1,272,512]{2,1,0:T(8,128)(2,1)S(1)} %get-tuple-element.109), channel_id=1, source_target_pairs={{0,1},{1,0},{2,3},{3,2},{4,5},{5,4},{6,7},{7,6},{8,9},{9,8},{10,11... | collective-permute-start | bytes 835592 | tf_op jit(solution)/shard_map/ppermute | solution.py:23
  209.0 26.8 %collective-permute-start.3 = (bf16[2,272,512]{2,1,0:T(8,128)(2,1)S(1)}, bf16[2,272,512]{2,1,0:T(8,128)(2,1)S(1)}, u32[]{:S(2)}, u32[]{:S(2)}) collective-permute-start(bf16[2,272,512]{2,1,0:T(8,128)(2,1)S(1)} %get-tuple-element.89), channel_id=1, source_target_pairs={{0,2},{1,3},{2,0},{3,1},{4,6},{5,7},{6,4},{7,5},{8,10},{9,11},{10,... | collective-permute-start | bytes 1671176 | tf_op jit(solution)/shard_map/ppermute | solution.py:23
  265.8 44.8 %all-gather.10.cloned.1.call-start = ((), (), s32[]{:S(2)}) async-start(), calls=%async_computation.10 | async-start | bytes 1310720 | tf_op jit(solution)/shard_map/all_gather | solution.py:101
  294.8 129.5 %reduce-scatter.12.cloned.1.call-start = ((), (), s32[]{:S(2)}) async-start(), calls=%async_computation.11 | async-start | bytes 1310720 | tf_op jit(solution)/shard_map/reduce_scatter | solution.py:99
  332.5 38.2 %copy-start.19 = (f32[8,4096]{1,0:T(8,128)}, f32[8,4096]{1,0:T(8,128)S(1)}, u32[]{:S(2)}) copy-start(f32[8,4096]{1,0:T(8,128)S(1)} %convolution_subtract_fusion.7) | copy-start | bytes 393220
  334.1 36.5 %copy-start.21 = (f32[8,4096]{1,0:T(8,128)}, f32[8,4096]{1,0:T(8,128)S(1)}, u32[]{:S(2)}) copy-start(f32[8,4096]{1,0:T(8,128)S(1)} %convolution_add_fusion.7) | copy-start | bytes 393220
  334.4 8.9 %collective-permute-start.4 = (bf16[1,272,512]{2,1,0:T(8,128)(2,1)S(1)}, bf16[1,272,512]{2,1,0:T(8,128)(2,1)S(1)}, u32[]{:S(2)}, u32[]{:S(2)}) collective-permute-start(bf16[1,272,512]{2,1,0:T(8,128)(2,1)S(1)} %get-tuple-element.107), channel_id=1, source_target_pairs={{0,1},{1,0},{2,3},{3,2},{4,5},{5,4},{6,7},{7,6},{8,9},{9,8},{10,11... | collective-permute-start | bytes 835592 | tf_op jit(solution)/shard_map/ppermute | solution.py:23
  343.5 26.8 %collective-permute-start.5 = (bf16[2,272,512]{2,1,0:T(8,128)(2,1)S(1)}, bf16[2,272,512]{2,1,0:T(8,128)(2,1)S(1)}, u32[]{:S(2)}, u32[]{:S(2)}) collective-permute-start(bf16[2,272,512]{2,1,0:T(8,128)(2,1)S(1)} %get-tuple-element.87), channel_id=1, source_target_pairs={{0,2},{1,3},{2,0},{3,1},{4,6},{5,7},{6,4},{7,5},{8,10},{9,11},{10,... | collective-permute-start | bytes 1671176 | tf_op jit(solution)/shard_map/ppermute | solution.py:23
  380.3 13.3 %slice-start.4 = ((s8[8388608]{0:T(1024)(128)(4,1)}), s8[4194304]{0:T(1024)(128)(4,1)S(1)}, s32[]{:S(2)}) async-start(s8[8388608]{0:T(1024)(128)(4,1)} %bitcast.478), calls=%async_computation.19 | async-start | bytes 8388608
  395.9 51.3 %copy-start.6 = (f32[32,4096]{1,0:T(8,128)S(1)}, f32[32,4096]{1,0:T(8,128)}, u32[]{:S(2)}) copy-start(f32[32,4096]{1,0:T(8,128)} %get-tuple-element.142) | copy-start | bytes 1572868
  397.1 44.8 %all-gather.12.cloned.1.call-start = ((), (), s32[]{:S(2)}) async-start(), calls=%async_computation.12 | async-start | bytes 1310720 | tf_op jit(solution)/shard_map/all_gather | solution.py:101
  426.1 128.4 %reduce-scatter.14.cloned.1.call-start = ((), (), s32[]{:S(2)}) async-start(), calls=%async_computation.13 | async-start | bytes 1310720 | tf_op jit(solution)/shard_map/reduce_scatter | solution.py:99
  451.1 21.1 %copy-start.4 = (f32[32,4096]{1,0:T(8,128)}, f32[32,4096]{1,0:T(8,128)S(1)}, u32[]{:S(2)}) copy-start(f32[32,4096]{1,0:T(8,128)S(1)} %get-tuple-element.143) | copy-start | bytes 1572868
  463.2 8.9 %collective-permute-start.6 = (bf16[1,272,512]{2,1,0:T(8,128)(2,1)S(1)}, bf16[1,272,512]{2,1,0:T(8,128)(2,1)S(1)}, u32[]{:S(2)}, u32[]{:S(2)}) collective-permute-start(bf16[1,272,512]{2,1,0:T(8,128)(2,1)S(1)} %get-tuple-element.105), channel_id=1, source_target_pairs={{0,1},{1,0},{2,3},{3,2},{4,5},{5,4},{6,7},{7,6},{8,9},{9,8},{10,11... | collective-permute-start | bytes 835592 | tf_op jit(solution)/shard_map/ppermute | solution.py:23
  472.2 31.3 %copy-start.2 = (bf16[4,272,512]{2,0,1:T(4,128)(2,1)S(1)}, bf16[4,272,512]{2,0,1:T(4,128)(2,1)}, u32[]{:S(2)}) copy-start(bf16[4,272,512]{2,0,1:T(4,128)(2,1)} %copy-done.1) | copy-start | bytes 3342340
  472.3 26.8 %collective-permute-start.7 = (bf16[2,272,512]{2,1,0:T(8,128)(2,1)S(1)}, bf16[2,272,512]{2,1,0:T(8,128)(2,1)S(1)}, u32[]{:S(2)}, u32[]{:S(2)}) collective-permute-start(bf16[2,272,512]{2,1,0:T(8,128)(2,1)S(1)} %get-tuple-element.85), channel_id=1, source_target_pairs={{0,2},{1,3},{2,0},{3,1},{4,6},{5,7},{6,4},{7,5},{8,10},{9,11},{10,... | collective-permute-start | bytes 1671176 | tf_op jit(solution)/shard_map/ppermute | solution.py:23
  510.4 13.3 %slice-start.6 = ((s8[8388608]{0:T(1024)(128)(4,1)}), s8[4194304]{0:T(1024)(128)(4,1)S(1)}, s32[]{:S(2)}) async-start(s8[8388608]{0:T(1024)(128)(4,1)} %bitcast.480), calls=%async_computation.21 | async-start | bytes 8388608
  526.1 51.1 %copy-start.5 = (f32[32,4096]{1,0:T(8,128)S(1)}, f32[32,4096]{1,0:T(8,128)}, u32[]{:S(2)}) copy-start(f32[32,4096]{1,0:T(8,128)} %copy-done.4) | copy-start | bytes 1572868
  526.1 51.1 %copy-start.11 = (f32[32,4096]{1,0:T(8,128)S(1)}, f32[32,4096]{1,0:T(8,128)}, u32[]{:S(2)}) copy-start(f32[32,4096]{1,0:T(8,128)} %get-tuple-element.76) | copy-start | bytes 1572868
  526.1 51.2 %copy-start.12 = (f32[32,4096]{1,0:T(8,128)S(1)}, f32[32,4096]{1,0:T(8,128)}, u32[]{:S(2)}) copy-start(f32[32,4096]{1,0:T(8,128)} %get-tuple-element.77) | copy-start | bytes 1572868
  527.2 44.7 %all-gather.14.cloned.1.call-start = ((), (), s32[]{:S(2)}) async-start(), calls=%async_computation.14 | async-start | bytes 1310720 | tf_op jit(solution)/shard_map/all_gather | solution.py:101
  591.0 15.1 %copy-start.16 = (f32[8,4096]{1,0:T(8,128)S(1)}, f32[8,4096]{1,0:T(8,128)}, u32[]{:S(2)}) copy-start(f32[8,4096]{1,0:T(8,128)} %copy-done.15) | copy-start | bytes 393220
  591.0 15.1 %copy-start.18 = (f32[8,4096]{1,0:T(8,128)S(1)}, f32[8,4096]{1,0:T(8,128)}, u32[]{:S(2)}) copy-start(f32[8,4096]{1,0:T(8,128)} %copy-done.17) | copy-start | bytes 393220
  591.0 15.2 %copy-start.20 = (f32[8,4096]{1,0:T(8,128)S(1)}, f32[8,4096]{1,0:T(8,128)}, u32[]{:S(2)}) copy-start(f32[8,4096]{1,0:T(8,128)} %copy-done.19) | copy-start | bytes 393220
  591.5 15.4 %copy-start.22 = (f32[8,4096]{1,0:T(8,128)S(1)}, f32[8,4096]{1,0:T(8,128)}, u32[]{:S(2)}) copy-start(f32[8,4096]{1,0:T(8,128)} %copy-done.21) | copy-start | bytes 393220
  592.9 8.9 %collective-permute-start.8 = (bf16[1,272,512]{2,1,0:T(8,128)(2,1)S(1)}, bf16[1,272,512]{2,1,0:T(8,128)(2,1)S(1)}, u32[]{:S(2)}, u32[]{:S(2)}) collective-permute-start(bf16[1,272,512]{2,1,0:T(8,128)(2,1)S(1)} %get-tuple-element.103), channel_id=1, source_target_pairs={{0,1},{1,0},{2,3},{3,2},{4,5},{5,4},{6,7},{7,6},{8,9},{9,8},{10,11... | collective-permute-start | bytes 835592 | tf_op jit(solution)/shard_map/ppermute | solution.py:23
  602.8 27.1 %collective-permute-start.9 = (bf16[2,272,512]{2,1,0:T(8,128)(2,1)}, bf16[2,272,512]{2,1,0:T(8,128)(2,1)}, u32[]{:S(2)}, u32[]{:S(2)}) collective-permute-start(bf16[2,272,512]{2,1,0:T(8,128)(2,1)} %get-tuple-element.83), channel_id=1, source_target_pairs={{0,2},{1,3},{2,0},{3,1},{4,6},{5,7},{6,4},{7,5},{8,10},{9,11},{10,... | collective-permute-start | bytes 1671176 | tf_op jit(solution)/shard_map/ppermute | solution.py:23
  606.1 28.1 %copy-start.10 = (f32[128,4,512]{2,1,0:T(4,128)S(1)}, f32[128,4,512]{2,1,0:T(4,128)}, u32[]{:S(2)}) copy-start(f32[128,4,512]{2,1,0:T(4,128)} %get-tuple-element.75) | copy-start | bytes 3145732
  645.5 40.4 %copy-start.36 = (f32[1,8,8,128]{3,2,1,0:T(8,128)S(1)}, f32[1,8,8,128]{3,2,1,0:T(8,128)}, u32[]{:S(2)}) copy-start(f32[1,8,8,128]{3,2,1,0:T(8,128)} %copy-done.35) | copy-start | bytes 98308
  645.5 40.5 %copy-start.38 = (f32[1,8,8,128]{3,2,1,0:T(8,128)S(1)}, f32[1,8,8,128]{3,2,1,0:T(8,128)}, u32[]{:S(2)}) copy-start(f32[1,8,8,128]{3,2,1,0:T(8,128)} %copy-done.37) | copy-start | bytes 98308
  645.5 40.5 %copy-start.40 = (f32[1,8,8,128]{3,2,1,0:T(8,128)S(1)}, f32[1,8,8,128]{3,2,1,0:T(8,128)}, u32[]{:S(2)}) copy-start(f32[1,8,8,128]{3,2,1,0:T(8,128)} %copy-done.39) | copy-start | bytes 98308
  645.5 40.4 %copy-start.42 = (f32[1,8,8,128]{3,2,1,0:T(8,128)S(1)}, f32[1,8,8,128]{3,2,1,0:T(8,128)}, u32[]{:S(2)}) copy-start(f32[1,8,8,128]{3,2,1,0:T(8,128)} %copy-done.41) | copy-start | bytes 98308
  645.5 42.0 %copy-start.29 = (f32[2,8,8,512]{3,2,1,0:T(8,128)S(1)}, f32[2,8,8,512]{3,2,1,0:T(8,128)}, u32[]{:S(2)}) copy-start(f32[2,8,8,512]{3,2,1,0:T(8,128)} %copy-done.28) | copy-start | bytes 786436
  645.5 42.0 %copy-start.30 = (f32[1,8,8,512]{3,2,1,0:T(8,128)S(1)}, f32[1,8,8,512]{3,2,1,0:T(8,128)}, u32[]{:S(2)}) copy-start(f32[1,8,8,512]{3,2,1,0:T(8,128)} %copy.39) | copy-start | bytes 393220
  645.5 42.0 %copy-start.31 = (f32[1,8,8,512]{3,2,1,0:T(8,128)S(1)}, f32[1,8,8,512]{3,2,1,0:T(8,128)}, u32[]{:S(2)}) copy-start(f32[1,8,8,512]{3,2,1,0:T(8,128)} %copy.38) | copy-start | bytes 393220
  645.6 42.0 %copy-start.32 = (f32[1,8,8,512]{3,2,1,0:T(8,128)S(1)}, f32[1,8,8,512]{3,2,1,0:T(8,128)}, u32[]{:S(2)}) copy-start(f32[1,8,8,512]{3,2,1,0:T(8,128)} %copy.43) | copy-start | bytes 393220
  645.6 42.0 %copy-start.33 = (f32[1,8,8,512]{3,2,1,0:T(8,128)S(1)}, f32[1,8,8,512]{3,2,1,0:T(8,128)}, u32[]{:S(2)}) copy-start(f32[1,8,8,512]{3,2,1,0:T(8,128)} %copy.42) | copy-start | bytes 393220
  645.6 42.0 %copy-start.34 = (f32[1,8,8,512]{3,2,1,0:T(8,128)S(1)}, f32[1,8,8,512]{3,2,1,0:T(8,128)}, u32[]{:S(2)}) copy-start(f32[1,8,8,512]{3,2,1,0:T(8,128)} %copy.45) | copy-start | bytes 393220
  (28 other events, 163.7 us)
Sparse Core Ops, SparseCore 0:
  17.1 29.8 reduce-scatter.5
  49.2 15.3 all-gather.5
  139.8 27.1 reduce-scatter.7
  169.0 15.3 all-gather.7
  266.0 27.1 reduce-scatter.9
  295.2 15.3 all-gather.9
  397.2 27.1 reduce-scatter.11
  426.5 15.3 all-gather.11
  527.3 27.1 reduce-scatter.13
  556.6 15.3 all-gather.13
